TPU v7x, 256 devices: a whole 4x4x8 slice. The times are simulated.
256 devices in a mesh: gx: 64 (over x, y, z_hi, core), gy: 4 (over z_lo).
Axes of the slice: x: 4, y: 4, z: 8 (z_hi: 2, z_lo: 4; z = z_hi * 4 + z_lo), core: 2. Of those that a mesh axis runs over, the one named last changes fastest.
Arguments:
- features: bfloat16 [64, 4, 2, 8, 8, 8, 128], P('gx', 'gy'), may hold values from -6 to 6
- cotangent: bfloat16 [64, 4, 2, 4, 4, 4, 256], P('gx', 'gy'), may hold values from -6 to 6
- conv_first: bfloat16 [27, 128, 128], replicated, may hold values from -0.109375 to 0.109375
- down_weight: bfloat16 [8, 128, 256], replicated, may hold values from -0.1875 to 0.1875
- conv_second: bfloat16 [27, 256, 256], replicated, may hold values from -0.078125 to 0.078125
- block_count: int32 [64, 4], P('gx', 'gy'), may hold values from 1 to 2, as said below
- neighbours: int32 [64, 4, 2, 26], P('gx', 'gy'), may hold values from -1 to 1, as said below
Outputs:
- output_field: bfloat16 [64, 4, 2, 4, 4, 4, 256], P('gx', 'gy')
- input_grad: bfloat16 [64, 4, 2, 8, 8, 8, 128], P('gx', 'gy')
- grad_first: float32 [27, 128, 128], P(None, 'gx')
- grad_down: float32 [8, 128, 256], P(None, 'gx')
- grad_second: float32 [27, 256, 256], P(None, 'gx')
Inputs may be any that keep to these rules, and one draw needn't show every extreme that they name: `block_count`: each column holds 1 to 2 active blocks at distinct levels of its 8, in slots 0 up to its count in rising level; some column holds exactly 2. neighbours[i, j, s, k] is the slot, in column (i + ox, j + oy), of the active block oz levels from slot s's block, for the k-th nonzero offset (ox, oy, oz) with ox slowest and oz fastest, or -1 where there is none; it is below that column's count; rows of slots at or past block_count[i, j] are all -1; the relation is symmetric.
All inputs are finite; a program needn't handle non-finite values.
Results may differ from a plain program's by a relative error of at most 0.01.
Values may be sent and summed in bfloat16 or wider, within the bound.
No kernel may reach another device: no remote copies, remote signals or barrier semaphores. Data moves between devices by JAX's collectives and lax.ppermute only.
A program may use at most 128 MiB of HBM per device.

v0:
```python
import math
import jax
import jax.numpy as jnp
from jax import lax
from jax.sharding import PartitionSpec as P

NEIGHBOUR_STEPS = (-1, 0, 1)


def as_sent(shard):
    return jax.tree.map(lambda a: a.astype(jnp.bfloat16) if a.dtype == jnp.float32 else a, shard)


def shifted(block, axis, distance):
    devices = range(lax.axis_size(axis))
    route = [(i - distance, i) for i in devices if i - distance in devices]
    return lax.ppermute(block, axis, route)


def column_of(offset_x, offset_y, offset_z):
    raster = 9 * (offset_x + 1) + 3 * (offset_y + 1) + (offset_z + 1)
    return raster - 1 if raster > 13 else raster


def outer_layer(values, axis, border):
    length = values.shape[axis]
    first_index = 0 if border == 0 else length - 1
    return lax.slice_in_dim(values, first_index, first_index + 1, axis=axis)


def share_faces(fields):
    nearby = [dict() for member in fields]
    onward = [dict() for member in fields]
    for stride in (1, -1):
        border = 1 if stride == 1 else 0
        payload = []
        for volume in fields:
            planar = outer_layer(volume, 1, border)
            payload += [planar, outer_layer(planar, 2, 0), outer_layer(planar, 2, 1)]
        arrived = shifted(as_sent(tuple(payload)), "gx", stride)
        member = 0
        nearby[member][-stride, 0] = arrived[3 * member]
        onward[member][-stride, 0] = arrived[3 * member + 1]
        onward[member][-stride, 1] = arrived[3 * member + 2]
    for stride in (1, -1):
        border = 1 if stride == 1 else 0
        payload = []
        member = 0
        payload += [
            outer_layer(fields[member], 2, border),
            onward[member][-1, border],
            onward[member][1, border],
        ]
        arrived = shifted(as_sent(tuple(payload)), "gy", stride)
        member = 0
        nearby[member][0, -stride] = arrived[3 * member]
        nearby[member][-1, -stride] = arrived[3 * member + 1]
        nearby[member][1, -stride] = arrived[3 * member + 2]
    return nearby


def surround(center, nearby, slot_table):
    depth = center.shape[3]
    slabs_x = []
    for offset_x in NEIGHBOUR_STEPS:
        slabs_y = []
        for offset_y in NEIGHBOUR_STEPS:
            source = center if offset_x == 0 and offset_y == 0 else nearby[offset_x, offset_y]
            pieces = []
            for offset_z in NEIGHBOUR_STEPS:
                if offset_x == 0 and offset_y == 0 and (offset_z == 0):
                    pieces.append(center)
                else:
                    slot_ids = slot_table[:, column_of(offset_x, offset_y, offset_z)]
                    picked = jnp.take(source, jnp.maximum(slot_ids, 0), axis=0)
                    picked = jnp.where(
                        (slot_ids >= 0)[:, None, None, None, None],
                        picked,
                        jnp.zeros((), picked.dtype),
                    )
                    if offset_z == -1:
                        picked = picked[:, :, :, depth - 1 :]
                    elif offset_z == 1:
                        picked = picked[:, :, :, :1]
                    pieces.append(picked)
            slabs_y.append(jnp.concatenate(pieces, axis=3))
        slabs_x.append(jnp.concatenate(slabs_y, axis=2))
    return jnp.concatenate(slabs_x, axis=1)


def unfold(padded, extent):
    windows = []
    for along_x in range(3):
        for along_y in range(3):
            for along_z in range(3):
                windows.append(
                    padded[
                        :,
                        along_x : along_x + extent,
                        along_y : along_y + extent,
                        along_z : along_z + extent,
                        :,
                    ]
                )
    stacked = jnp.concatenate(windows, axis=-1)
    return stacked.reshape(-1, stacked.shape[-1])


def into_cells(blocks, half_edge):
    slot_count, channels = (blocks.shape[0], blocks.shape[-1])
    lattice = blocks.reshape(slot_count, half_edge, 2, half_edge, 2, half_edge, 2, channels)
    lattice = lattice.transpose(0, 1, 3, 5, 2, 4, 6, 7)
    return lattice.reshape(slot_count * half_edge**3, 8 * channels)


def from_cells(cell_rows, slot_count, half_edge, channels):
    lattice = cell_rows.reshape(slot_count, half_edge, half_edge, half_edge, 2, 2, 2, channels)
    lattice = lattice.transpose(0, 1, 4, 2, 5, 3, 6, 7)
    return lattice.reshape(slot_count, 2 * half_edge, 2 * half_edge, 2 * half_edge, channels)


def silu_slope(values):
    logistic = jax.nn.sigmoid(values)
    return logistic * (1.0 + values * (1.0 - logistic))


def contract_rows(left, right):
    return lax.dot_general(
        left, right, (((0,), (0,)), ((), ())), preferred_element_type=jnp.float32
    )


def body(features, cotangent, conv_first, down_weight, conv_second, block_count, neighbours):
    inputs = features[0, 0]
    slot_count, extent, channels = (inputs.shape[0], inputs.shape[1], inputs.shape[-1])
    half_edge = extent // 2
    wide_channels = conv_second.shape[-1]
    slot_table = neighbours[0, 0]
    live_mask = (jnp.arange(slot_count) < block_count[0, 0])[:, None, None, None, None]
    inputs = jnp.where(live_mask, inputs, jnp.zeros((), inputs.dtype))
    seed_blocks = jnp.where(live_mask, cotangent[0, 0], jnp.zeros((), inputs.dtype))
    near_input = share_faces((inputs,))[0]
    first_matrix = conv_first.reshape(-1, channels)
    first_cols = unfold(surround(inputs, near_input, slot_table), extent)
    pre_first = jnp.dot(first_cols, first_matrix, preferred_element_type=jnp.float32)
    hidden_first = jax.nn.silu(pre_first).astype(jnp.bfloat16)
    first_cells = into_cells(
        hidden_first.reshape(slot_count, extent, extent, extent, channels), half_edge
    )
    down_matrix = down_weight.reshape(-1, wide_channels)
    pre_down = jnp.dot(first_cells, down_matrix, preferred_element_type=jnp.float32)
    hidden_down = (
        jax.nn.silu(pre_down)
        .astype(jnp.bfloat16)
        .reshape(slot_count, half_edge, half_edge, half_edge, wide_channels)
    )
    near_hidden = share_faces((hidden_down,))[0]
    second_cols = unfold(surround(hidden_down, near_hidden, slot_table), half_edge)
    second_matrix = conv_second.reshape(-1, wide_channels)
    output_field = jnp.dot(second_cols, second_matrix, preferred_element_type=jnp.float32).astype(
        jnp.bfloat16
    )
    near_seed = share_faces((seed_blocks,))[0]
    seed_cols = unfold(surround(seed_blocks, near_seed, slot_table), half_edge)
    second_flip = jnp.transpose(conv_second[::-1], (0, 2, 1)).reshape(-1, wide_channels)
    back_down = jnp.dot(seed_cols, second_flip, preferred_element_type=jnp.float32)
    delta_down = (back_down * silu_slope(pre_down)).astype(jnp.bfloat16)
    grad_second = contract_rows(second_cols, seed_blocks.reshape(-1, wide_channels))
    grad_down = contract_rows(first_cells, delta_down)
    back_cells = lax.dot_general(
        delta_down, down_matrix, (((1,), (1,)), ((), ())), preferred_element_type=jnp.float32
    )
    back_first = from_cells(back_cells, slot_count, half_edge, channels).reshape(-1, channels)
    delta_first = (back_first * silu_slope(pre_first)).astype(jnp.bfloat16)
    delta_blocks = delta_first.reshape(slot_count, extent, extent, extent, channels)
    near_delta = share_faces((delta_blocks,))[0]
    delta_cols = unfold(surround(delta_blocks, near_delta, slot_table), extent)
    first_flip = jnp.transpose(conv_first[::-1], (0, 2, 1)).reshape(-1, channels)
    input_grad = jnp.dot(delta_cols, first_flip, preferred_element_type=jnp.float32).astype(
        jnp.bfloat16
    )
    grad_first = contract_rows(first_cols, delta_first)
    first_term = grad_first.reshape(27, channels, channels)
    down_term = grad_down.reshape(8, channels, wide_channels)
    second_term = grad_second.reshape(27, wide_channels, wide_channels)
    columns = (
        lax.psum_scatter(first_term, "gx", scatter_dimension=1, tiled=True),
        lax.psum_scatter(down_term, "gx", scatter_dimension=1, tiled=True),
        lax.psum_scatter(second_term, "gx", scatter_dimension=1, tiled=True),
    )
    summed = (
        lax.psum(columns[0].astype(jnp.bfloat16), "gy").astype(jnp.float32),
        lax.psum(columns[1].astype(jnp.bfloat16), "gy").astype(jnp.float32),
        lax.psum(columns[2].astype(jnp.bfloat16), "gy").astype(jnp.float32),
    )
    devices = lax.axis_size("gx") * lax.axis_size("gy")
    scale_first = 1.0 / math.sqrt(float(devices * slot_count * extent**3))
    scale_half = 1.0 / math.sqrt(float(devices * slot_count * half_edge**3))
    return (
        output_field.reshape(1, 1, slot_count, half_edge, half_edge, half_edge, wide_channels),
        input_grad.reshape(1, 1, slot_count, extent, extent, extent, channels),
        summed[0] * scale_first,
        summed[1] * scale_half,
        summed[2] * scale_half,
    )


def solution(mesh):
    placed = (
        P("gx", "gy", None, None, None, None, None),
        P("gx", "gy", None, None, None, None, None),
        P(),
        P(),
        P(),
        P("gx", "gy"),
        P("gx", "gy", None, None),
    )
    return jax.shard_map(
        body,
        mesh=mesh,
        in_specs=placed,
        out_specs=(
            P("gx", "gy", None, None, None, None, None),
            P("gx", "gy", None, None, None, None, None),
            P(None, "gx", None),
            P(None, "gx", None),
            P(None, "gx", None),
        ),
        check_vma=False,
    )
```

profile of v0, /device:TPU:2, one launch (start us, length us, event | category | flops | bytes accessed | tf_op | source)
XLA Modules:
  0.0 1120.0 jit_solution(13349509447897729206)
XLA Ops:
  10.9 9.2 collective-permute-start
  27.4 7.5 collective-permute-start.31
  63.4 4.3 collective-permute-start.1
  73.2 5.7 copy.23
  79.0 4.2 rev.6
  89.1 4.5 collective-permute-start.29
  114.8 9.1 collective-permute-start.33
  126.5 5.5 collective-permute-start.25
  134.7 4.6 collective-permute-start.5
  141.2 10.6 collective-permute-start.9
  194.7 10.3 copy.26
  205.0 3.9 collective-permute-start.17
  208.9 10.3 collective-permute-start.19
  226.4 3.9 collective-permute-start.20
  240.9 8.6 collective-permute-start.21
  326.5 5.0 fusion.3
  386.0 5.4 fusion.61
  392.7 10.6 collective-permute-start.43
  409.6 7.5 collective-permute-start.39
  420.4 547.1 %all-reduce.8 = (bf16[27,128,128]{2,1,0:T(8,128)(2,1)}, bf16[27,256,256]{2,1,0:T(8,128)(2,1)}) all-reduce(f32[27,128,128]{2,1,0:T(8,128)S(1)} %fusion.3, f32[27,256,256]{2,1,0:T(8,128)} %fusion.61), channel_id=2, replica_groups=mesh['gx'=64,'gy'=4] {'gx'}, use_global_device_ids=true, to_apply=%region_0.9.clone | all-reduce | flops 2211840 | bytes 13271040
  973.1 15.6 %collective-permute-start.37 = (bf16[2,1,1,8,128]{4,3,2,1,0:T(8,128)(2,1)S(1)}, bf16[2,1,1,8,128]{4,3,2,1,0:T(8,128)(2,1)S(1)}, u32[]{:S(2)}, u32[]{:S(2)}) collective-permute-start(bf16[2,1,1,8,128]{4,3,2,1,0:T(8,128)(2,1)S(1)} %collective-permute-done.36), channel_id=1, source_target_pairs={{0,1},{1,2},{2,3},{4,5},{5,6},{6,7},{8,9},{9,10},{10,11},{12,13},{... | collective-permute-start | bytes 12296 | tf_op jit(solution)/shard_map/ppermute | solution.py:17
  992.2 4.5 collective-permute-start.41
  1051.4 5.8 convolution_convert_fusion
  1057.1 51.8 %all-reduce.7.cloned.1.call-done = (bf16[27,2,128]{2,1,0:T(2,128)(2,1)}, bf16[8,2,256]{2,0,1:T(8,128)(2,1)}, bf16[27,4,256]{2,1,0:T(4,128)(2,1)}) async-done(((bf16[27,2,128]{2,1,0:T(2,128)(2,1)}, bf16[8,2,256]{2,0,1:T(8,128)(2,1)}, bf16[27,4,256]{2,1,0:T(4,128)(2,1)}), (bf16[27,2,128]{2,1,0:T(2,128)(2,1)}, bf16[8,2,256]{2,0,1:T(8,128)(2,1)}, bf16[27,4,256]{2,1,0:T(4,128)(2,1)})) %all-reduce.7.cloned.1.call-update) | async-done | bytes 77328 | tf_op jit(solution)/shard_map/psum | solution.py:192
  (759 shorter events, 345.5 us)
Async XLA Ops:
  7.2 1042.8 %reduce-scatter.4.cloned.1.call-start = ((), (), s32[]{:S(2)}) async-start(), calls=%async_computation.1 | async-start | bytes 1064960 | tf_op jit(solution)/shard_map/reduce_scatter | solution.py:188
  9.0 50.6 %collective-permute-start.3 = (bf16[2,1,1,8,128]{4,3,2,1,0:T(8,128)(2,1)S(1)}, bf16[2,1,1,8,128]{4,3,2,1,0:T(8,128)(2,1)S(1)}, u32[]{:S(2)}, u32[]{:S(2)}) collective-permute-start(bf16[2,1,1,8,128]{4,3,2,1,0:T(8,128)(2,1)S(1)} %get-tuple-element.115), channel_id=1, source_target_pairs={{0,4},{4,8},{8,12},{12,16},{16,20},{20,24},{24,28},{28,32},{32,36}... | collective-permute-start | bytes 12296 | tf_op jit(solution)/shard_map/ppermute | solution.py:17
  10.9 50.0 %collective-permute-start = (bf16[2,1,1,8,128]{4,3,2,1,0:T(8,128)(2,1)S(1)}, bf16[2,1,1,8,128]{4,3,2,1,0:T(8,128)(2,1)S(1)}, u32[]{:S(2)}, u32[]{:S(2)}) collective-permute-start(bf16[2,1,1,8,128]{4,3,2,1,0:T(8,128)(2,1)S(1)} %get-tuple-element.116), channel_id=1, source_target_pairs={{0,4},{4,8},{8,12},{12,16},{16,20},{20,24},{24,28},{28,32},{32,36}... | collective-permute-start | bytes 12296 | tf_op jit(solution)/shard_map/ppermute | solution.py:17
  20.1 43.2 %collective-permute-start.7 = (bf16[2,1,1,8,128]{4,3,2,1,0:T(8,128)(2,1)S(1)}, bf16[2,1,1,8,128]{4,3,2,1,0:T(8,128)(2,1)S(1)}, u32[]{:S(2)}, u32[]{:S(2)}) collective-permute-start(bf16[2,1,1,8,128]{4,3,2,1,0:T(8,128)(2,1)S(1)} %get-tuple-element.113), channel_id=1, source_target_pairs={{4,0},{8,4},{12,8},{16,12},{20,16},{24,20},{28,24},{32,28},{36,32}... | collective-permute-start | bytes 12296 | tf_op jit(solution)/shard_map/ppermute | solution.py:17
  23.8 43.8 %collective-permute-start.10 = (bf16[2,1,1,8,128]{4,3,2,1,0:T(8,128)(2,1)S(1)}, bf16[2,1,1,8,128]{4,3,2,1,0:T(8,128)(2,1)S(1)}, u32[]{:S(2)}, u32[]{:S(2)}) collective-permute-start(bf16[2,1,1,8,128]{4,3,2,1,0:T(8,128)(2,1)S(1)} %get-tuple-element.114), channel_id=1, source_target_pairs={{4,0},{8,4},{12,8},{16,12},{20,16},{24,20},{28,24},{32,28},{36,32}... | collective-permute-start | bytes 12296 | tf_op jit(solution)/shard_map/ppermute | solution.py:17
  27.4 71.0 %collective-permute-start.31 = (bf16[2,1,1,4,256]{4,3,2,1,0:T(4,128)(2,1)S(1)}, bf16[2,1,1,4,256]{4,3,2,1,0:T(4,128)(2,1)S(1)}, u32[]{:S(2)}, u32[]{:S(2)}) collective-permute-start(bf16[2,1,1,4,256]{4,3,2,1,0:T(4,128)(2,1)S(1)} %get-tuple-element.149), channel_id=1, source_target_pairs={{4,0},{8,4},{12,8},{16,12},{20,16},{24,20},{28,24},{32,28},{36,32}... | collective-permute-start | bytes 12296 | tf_op jit(solution)/shard_map/ppermute | solution.py:17
  61.0 39.9 %collective-permute-start.34 = (bf16[2,1,1,4,256]{4,3,2,1,0:T(4,128)(2,1)S(1)}, bf16[2,1,1,4,256]{4,3,2,1,0:T(4,128)(2,1)S(1)}, u32[]{:S(2)}, u32[]{:S(2)}) collective-permute-start(bf16[2,1,1,4,256]{4,3,2,1,0:T(4,128)(2,1)S(1)} %get-tuple-element.150), channel_id=1, source_target_pairs={{4,0},{8,4},{12,8},{16,12},{20,16},{24,20},{28,24},{32,28},{36,32}... | collective-permute-start | bytes 12296 | tf_op jit(solution)/shard_map/ppermute | solution.py:17
  70.6 33.9 %collective-permute-start.11 = (bf16[2,1,1,8,128]{4,3,2,1,0:T(8,128)(2,1)S(1)}, bf16[2,1,1,8,128]{4,3,2,1,0:T(8,128)(2,1)S(1)}, u32[]{:S(2)}, u32[]{:S(2)}) collective-permute-start(bf16[2,1,1,8,128]{4,3,2,1,0:T(8,128)(2,1)S(1)} %collective-permute-done.10), channel_id=1, source_target_pairs={{1,0},{2,1},{3,2},{5,4},{6,5},{7,6},{9,8},{10,9},{11,10},{13,12},{... | collective-permute-start | bytes 12296 | tf_op jit(solution)/shard_map/ppermute | solution.py:17
  89.1 50.1 %collective-permute-start.29 = (bf16[2,4,1,4,256]{4,3,2,1,0:T(4,128)(2,1)S(1)}, bf16[2,4,1,4,256]{4,3,2,1,0:T(4,128)(2,1)S(1)}, u32[]{:S(2)}, u32[]{:S(2)}) collective-permute-start(bf16[2,4,1,4,256]{4,3,2,1,0:T(4,128)(2,1)S(1)} %get-tuple-element.155), channel_id=1, source_target_pairs={{0,1},{1,2},{2,3},{4,5},{5,6},{6,7},{8,9},{9,10},{10,11},{12,13},{... | collective-permute-start | bytes 49160 | tf_op jit(solution)/shard_map/ppermute | solution.py:17
  133.4 35.1 %collective-permute-start.6 = (bf16[2,8,1,8,128]{4,3,2,1,0:T(8,128)(2,1)S(1)}, bf16[2,8,1,8,128]{4,3,2,1,0:T(8,128)(2,1)S(1)}, u32[]{:S(2)}, u32[]{:S(2)}) collective-permute-start(bf16[2,8,1,8,128]{4,3,2,1,0:T(8,128)(2,1)S(1)} %get-tuple-element.120), channel_id=1, source_target_pairs={{1,0},{2,1},{3,2},{5,4},{6,5},{7,6},{9,8},{10,9},{11,10},{13,12},{... | collective-permute-start | bytes 98312 | tf_op jit(solution)/shard_map/ppermute | solution.py:17
  134.7 35.5 %collective-permute-start.5 = (bf16[2,8,1,8,128]{4,3,2,1,0:T(8,128)(2,1)S(1)}, bf16[2,8,1,8,128]{4,3,2,1,0:T(8,128)(2,1)S(1)}, u32[]{:S(2)}, u32[]{:S(2)}) collective-permute-start(bf16[2,8,1,8,128]{4,3,2,1,0:T(8,128)(2,1)S(1)} %get-tuple-element.119), channel_id=1, source_target_pairs={{0,1},{1,2},{2,3},{4,5},{5,6},{6,7},{8,9},{9,10},{10,11},{12,13},{... | collective-permute-start | bytes 98312 | tf_op jit(solution)/shard_map/ppermute | solution.py:17
  139.3 32.6 %collective-permute-start.2 = (bf16[2,1,8,8,128]{4,3,2,1,0:T(8,128)(2,1)S(1)}, bf16[2,1,8,8,128]{4,3,2,1,0:T(8,128)(2,1)S(1)}, u32[]{:S(2)}, u32[]{:S(2)}) collective-permute-start(bf16[2,1,8,8,128]{4,3,2,1,0:T(8,128)(2,1)S(1)} %get-tuple-element.118), channel_id=1, source_target_pairs={{0,4},{4,8},{8,12},{12,16},{16,20},{20,24},{24,28},{28,32},{32,36}... | collective-permute-start | bytes 98312 | tf_op jit(solution)/shard_map/ppermute | solution.py:17
  141.2 32.4 %collective-permute-start.9 = (bf16[2,1,8,8,128]{4,3,2,1,0:T(8,128)(2,1)S(1)}, bf16[2,1,8,8,128]{4,3,2,1,0:T(8,128)(2,1)S(1)}, u32[]{:S(2)}, u32[]{:S(2)}) collective-permute-start(bf16[2,1,8,8,128]{4,3,2,1,0:T(8,128)(2,1)S(1)} %get-tuple-element.117), channel_id=1, source_target_pairs={{4,0},{8,4},{12,8},{16,12},{20,16},{24,20},{28,24},{32,28},{36,32}... | collective-permute-start | bytes 98312 | tf_op jit(solution)/shard_map/ppermute | solution.py:17
  205.0 72.1 %collective-permute-start.17 = (bf16[2,4,1,4,256]{4,3,2,1,0:T(4,128)(2,1)S(1)}, bf16[2,4,1,4,256]{4,3,2,1,0:T(4,128)(2,1)S(1)}, u32[]{:S(2)}, u32[]{:S(2)}) collective-permute-start(bf16[2,4,1,4,256]{4,3,2,1,0:T(4,128)(2,1)S(1)} %get-tuple-element.165), channel_id=1, source_target_pairs={{0,1},{1,2},{2,3},{4,5},{5,6},{6,7},{8,9},{9,10},{10,11},{12,13},{... | collective-permute-start | bytes 49160 | tf_op jit(solution)/shard_map/ppermute | solution.py:17
  240.9 38.3 %collective-permute-start.21 = (bf16[2,1,4,4,256]{4,3,2,1,0:T(4,128)(2,1)S(1)}, bf16[2,1,4,4,256]{4,3,2,1,0:T(4,128)(2,1)S(1)}, u32[]{:S(2)}, u32[]{:S(2)}) collective-permute-start(bf16[2,1,4,4,256]{4,3,2,1,0:T(4,128)(2,1)S(1)} %get-tuple-element.161), channel_id=1, source_target_pairs={{4,0},{8,4},{12,8},{16,12},{20,16},{24,20},{28,24},{32,28},{36,32}... | collective-permute-start | bytes 49160 | tf_op jit(solution)/shard_map/ppermute | solution.py:17
  251.6 29.8 %collective-permute-start.18 = (bf16[2,4,1,4,256]{4,3,2,1,0:T(4,128)(2,1)S(1)}, bf16[2,4,1,4,256]{4,3,2,1,0:T(4,128)(2,1)S(1)}, u32[]{:S(2)}, u32[]{:S(2)}) collective-permute-start(bf16[2,4,1,4,256]{4,3,2,1,0:T(4,128)(2,1)S(1)} %get-tuple-element.166), channel_id=1, source_target_pairs={{1,0},{2,1},{3,2},{5,4},{6,5},{7,6},{9,8},{10,9},{11,10},{13,12},{... | collective-permute-start | bytes 49160 | tf_op jit(solution)/shard_map/ppermute | solution.py:17
  255.0 28.2 %collective-permute-start.14 = (bf16[2,1,4,4,256]{4,3,2,1,0:T(4,128)(2,1)S(1)}, bf16[2,1,4,4,256]{4,3,2,1,0:T(4,128)(2,1)S(1)}, u32[]{:S(2)}, u32[]{:S(2)}) collective-permute-start(bf16[2,1,4,4,256]{4,3,2,1,0:T(4,128)(2,1)S(1)} %get-tuple-element.162), channel_id=1, source_target_pairs={{0,4},{4,8},{8,12},{12,16},{16,20},{20,24},{24,28},{28,32},{32,36}... | collective-permute-start | bytes 49160 | tf_op jit(solution)/shard_map/ppermute | solution.py:17
  392.7 716.3 %all-reduce.7.cloned.1.call-start = ((), (), s32[]{:S(2)}) async-start(), calls=%async_computation.2 | async-start | bytes 154624 | tf_op jit(solution)/shard_map/psum | solution.py:192
  392.7 577.8 %collective-permute-start.43 = (bf16[2,1,1,8,128]{4,3,2,1,0:T(8,128)(2,1)S(1)}, bf16[2,1,1,8,128]{4,3,2,1,0:T(8,128)(2,1)S(1)}, u32[]{:S(2)}, u32[]{:S(2)}) collective-permute-start(bf16[2,1,1,8,128]{4,3,2,1,0:T(8,128)(2,1)S(1)} %copy-done.110), channel_id=1, source_target_pairs={{4,0},{8,4},{12,8},{16,12},{20,16},{24,20},{28,24},{32,28},{36,32}... | collective-permute-start | bytes 12296 | tf_op jit(solution)/shard_map/ppermute | solution.py:17
  403.3 609.4 %collective-permute-start.45 = (bf16[2,1,8,8,128]{4,3,2,1,0:T(8,128)(2,1)S(1)}, bf16[2,1,8,8,128]{4,3,2,1,0:T(8,128)(2,1)S(1)}, u32[]{:S(2)}, u32[]{:S(2)}) collective-permute-start(bf16[2,1,8,8,128]{4,3,2,1,0:T(8,128)(2,1)S(1)} %copy-done.33), channel_id=1, source_target_pairs={{4,0},{8,4},{12,8},{16,12},{20,16},{24,20},{28,24},{32,28},{36,32}... | collective-permute-start | bytes 98312 | tf_op jit(solution)/shard_map/ppermute | solution.py:17
  405.2 566.6 %collective-permute-start.46 = (bf16[2,1,1,8,128]{4,3,2,1,0:T(8,128)(2,1)S(1)}, bf16[2,1,1,8,128]{4,3,2,1,0:T(8,128)(2,1)S(1)}, u32[]{:S(2)}, u32[]{:S(2)}) collective-permute-start(bf16[2,1,1,8,128]{4,3,2,1,0:T(8,128)(2,1)S(1)} %copy-done.109), channel_id=1, source_target_pairs={{4,0},{8,4},{12,8},{16,12},{20,16},{24,20},{28,24},{32,28},{36,32}... | collective-permute-start | bytes 12296 | tf_op jit(solution)/shard_map/ppermute | solution.py:17
  407.2 565.9 %collective-permute-start.36 = (bf16[2,1,1,8,128]{4,3,2,1,0:T(8,128)(2,1)S(1)}, bf16[2,1,1,8,128]{4,3,2,1,0:T(8,128)(2,1)S(1)}, u32[]{:S(2)}, u32[]{:S(2)}) collective-permute-start(bf16[2,1,1,8,128]{4,3,2,1,0:T(8,128)(2,1)S(1)} %copy-done.108), channel_id=1, source_target_pairs={{0,4},{4,8},{8,12},{12,16},{16,20},{20,24},{24,28},{28,32},{32,36}... | collective-permute-start | bytes 12296 | tf_op jit(solution)/shard_map/ppermute | solution.py:17
  409.6 579.2 %collective-permute-start.39 = (bf16[2,1,1,8,128]{4,3,2,1,0:T(8,128)(2,1)S(1)}, bf16[2,1,1,8,128]{4,3,2,1,0:T(8,128)(2,1)S(1)}, u32[]{:S(2)}, u32[]{:S(2)}) collective-permute-start(bf16[2,1,1,8,128]{4,3,2,1,0:T(8,128)(2,1)S(1)} %copy-done.107), channel_id=1, source_target_pairs={{0,4},{4,8},{8,12},{12,16},{16,20},{20,24},{24,28},{28,32},{32,36}... | collective-permute-start | bytes 12296 | tf_op jit(solution)/shard_map/ppermute | solution.py:17
  973.1 29.0 %collective-permute-start.37 = (bf16[2,1,1,8,128]{4,3,2,1,0:T(8,128)(2,1)S(1)}, bf16[2,1,1,8,128]{4,3,2,1,0:T(8,128)(2,1)S(1)}, u32[]{:S(2)}, u32[]{:S(2)}) collective-permute-start(bf16[2,1,1,8,128]{4,3,2,1,0:T(8,128)(2,1)S(1)} %collective-permute-done.36), channel_id=1, source_target_pairs={{0,1},{1,2},{2,3},{4,5},{5,6},{6,7},{8,9},{9,10},{10,11},{12,13},{... | collective-permute-start | bytes 12296 | tf_op jit(solution)/shard_map/ppermute | solution.py:17
  (138 other events, 10832.8 us)
Sparse Core Ops, SparseCore 0:
  392.8 414.3 reduce-scatter.3
  1051.5 57.4 all-reduce.6
where the time goes:
time: 1120 us
  blocking collectives  547 us (49%)
  local copies, waits for them, and re-layouts  194 us (17%)
  starting transfers between devices  183 us (16%)
  other arithmetic  95.3 us (9%)
  waiting for transfers between devices  54.4 us (5%)
  matrix products  26.9 us (2%)
  between operations  19 us (2%)
    unnamed x1, blocking collectives  547 us
    ppermute x48, starting transfers between devices, shifted(): return lax.ppermute(block, axis, route)  183 us
    unnamed x326, local copies, waits for them, and re-layouts  76.4 us
    gather x104, local copies, waits for them, and re-layouts, surround(): picked = jnp.take(source, jnp.maximum(slot_ids, 0), axis=0)  65.7 us
    select_n x66, other arithmetic, surround(): jnp.where((slot_ids >= 0)[:, None, None, None, None], picked, jnp.zeros((...  57.1 us
    psum x1, waiting for transfers between devices, body(): lax.psum(columns[0].astype(jnp.bfloat16), 'gy').astype(jnp.float32)  51.8 us
  transfers between devices with their start and end apart: 50, of which 3 were waited for; matrix products, arithmetic and copies ran while one was open for 15% of the time, Pallas kernels for 0%

commit v1 on v0

--- a/solution.py
+++ b/solution.py
@@ -3,8 +3,13 @@
 import jax.numpy as jnp
 from jax import lax
 from jax.sharding import PartitionSpec as P
+from jax.lax import all_gather
 
 NEIGHBOUR_STEPS = (-1, 0, 1)
+
+
+def _follow_screen(base_x):
+    return jnp.sum(all_gather(base_x, axis_name="gy"), 0)
 
 
 def as_sent(shard):
@@ -189,7 +194,7 @@
         lax.psum_scatter(second_term, "gx", scatter_dimension=1, tiled=True),
     )
     summed = (
-        lax.psum(columns[0].astype(jnp.bfloat16), "gy").astype(jnp.float32),
+        _follow_screen(columns[0].astype(jnp.bfloat16)).astype(jnp.float32),
         lax.psum(columns[1].astype(jnp.bfloat16), "gy").astype(jnp.float32),
         lax.psum(columns[2].astype(jnp.bfloat16), "gy").astype(jnp.float32),
     )

time: 1120 us -> 1090 us (0.973)
  blocking collectives: 547 us -> 599 us
  waiting for transfers between devices: 54.4 us -> 2.54 us
  local copies, waits for them, and re-layouts: 194 us -> 175 us
  starting transfers between devices: 183 us -> 169 us
    psum x1 -> x0, waiting for transfers between devices: 51.8 us -> none  [body(): lax.psum(columns[0].astype(jnp.bfloat16), 'gy').astype(jnp.float32)]
    all_gather x0 -> x1, blocking collectives: none -> 23.3 us  [_follow_screen(): return jnp.sum(all_gather(base_x, axis_name='gy'), 0)]
    psum x0 -> x1, blocking collectives: none -> 20.9 us  [body(): lax.psum(columns[1].astype(jnp.bfloat16), 'gy').astype(jnp.float32)]
    unnamed x326, local copies, waits for them, and re-layouts: 76.4 us -> 59 us
    ppermute x48, starting transfers between devices: 183 us -> 169 us  [shifted(): return lax.ppermute(block, axis, route)]
  transfers between devices with their start and end apart: 50 -> 49, of which waited for: 3 -> 2; matrix products, arithmetic and copies ran while one was open for 15% -> 14% of each run, Pallas kernels for 0% -> 0%
where the time goes in v1:
time: 1090 us; the launch traced here: 1080 us
  blocking collectives  599 us (55%)
  local copies, waits for them, and re-layouts  175 us (16%)
  starting transfers between devices  169 us (16%)
  other arithmetic  93.1 us (9%)
  matrix products  23.7 us (2%)
  between operations  19.5 us (2%)
    unnamed x1, blocking collectives  554 us
    ppermute x48, starting transfers between devices, shifted(): return lax.ppermute(block, axis, route)  169 us
    gather x104, local copies, waits for them, and re-layouts, surround(): picked = jnp.take(source, jnp.maximum(slot_ids, 0), axis=0)  65.7 us
    unnamed x326, local copies, waits for them, and re-layouts  59 us
    select_n x66, other arithmetic, surround(): jnp.where((slot_ids >= 0)[:, None, None, None, None], picked, jnp.zeros((...  57.4 us
    all_gather x1, blocking collectives, _follow_screen(): return jnp.sum(all_gather(base_x, axis_name='gy'), 0)  23.3 us
  transfers between devices with their start and end apart: 49, of which 2 were waited for; matrix products, arithmetic and copies ran while one was open for 14% of the time, Pallas kernels for 0%

profile of v1, /device:TPU:2, one launch (start us, length us, event | category | flops | bytes accessed | tf_op | source)
XLA Modules:
  0.0 1081.1 jit_solution(12026432976370951578)
XLA Ops:
  10.9 9.2 collective-permute-start
  27.4 7.5 collective-permute-start.31
  63.6 4.3 collective-permute-start.1
  73.4 5.7 copy.23
  79.2 4.2 rev.6
  89.3 4.5 collective-permute-start.29
  115.1 9.1 collective-permute-start.33
  126.8 5.5 collective-permute-start.25
  134.9 4.6 collective-permute-start.5
  141.4 10.6 collective-permute-start.9
  195.3 10.3 copy.26
  205.6 3.9 collective-permute-start.17
  209.6 10.3 collective-permute-start.19
  227.1 3.9 collective-permute-start.20
  241.6 8.6 collective-permute-start.21
  327.2 5.0 fusion.3
  386.6 5.3 fusion.61
  393.3 554.4 %all-reduce.5 = (bf16[27,128,128]{2,1,0:T(8,128)(2,1)}, bf16[27,256,256]{2,1,0:T(8,128)(2,1)}) all-reduce(f32[27,128,128]{2,1,0:T(8,128)S(1)} %fusion.3, f32[27,256,256]{2,1,0:T(8,128)} %fusion.61), channel_id=3, replica_groups=mesh['gx'=64,'gy'=4] {'gx'}, use_global_device_ids=true, to_apply=%region_0.9.clone | all-reduce | flops 2211840 | bytes 13271040
  948.6 23.3 %all-gather = bf16[108,2,128]{2,1,0:T(2,128)(2,1)S(1)} all-gather(bf16[27,2,128]{2,1,0:T(2,128)(2,1)S(1)} %dynamic-slice_convert_fusion.1), channel_id=2, replica_groups=mesh['gx'=64,'gy'=4] {'gy'}, dimensions={0}, use_global_device_ids=true | all-gather | bytes 69120 | tf_op jit(solution)/shard_map/all_gather | solution.py:12
  972.6 4.9 collective-permute-start.43
  983.8 7.5 collective-permute-start.39
  1000.7 4.5 collective-permute-start.37
  1008.2 4.5 collective-permute-start.41
  1051.9 20.9 %all-reduce.3 = (bf16[8,2,256]{2,0,1:T(8,128)(2,1)S(1)}, bf16[27,4,256]{2,1,0:T(4,128)(2,1)S(1)}) all-reduce(bf16[8,2,256]{2,0,1:T(8,128)(2,1)S(1)} %convert_element_type.46, bf16[27,4,256]{2,1,0:T(4,128)(2,1)S(1)} %dynamic-slice_convert_fusion), channel_id=1, replica_groups=mesh['gx'=64,'gy'=4] {'gy'}, use_global_device_ids=true, to_apply=%region_3.12 | all-reduce | flops 31744 | bytes 126976 | tf_op jit(solution)/shard_map/psum | solution.py:198
  (759 shorter events, 328.9 us)
Async XLA Ops:
  7.2 1043.9 %reduce-scatter.4.cloned.1.call-start = ((), (), s32[]{:S(2)}) async-start(), calls=%async_computation.1 | async-start | bytes 1064960 | tf_op jit(solution)/shard_map/reduce_scatter | solution.py:193
  9.0 50.8 %collective-permute-start.3 = (bf16[2,1,1,8,128]{4,3,2,1,0:T(8,128)(2,1)S(1)}, bf16[2,1,1,8,128]{4,3,2,1,0:T(8,128)(2,1)S(1)}, u32[]{:S(2)}, u32[]{:S(2)}) collective-permute-start(bf16[2,1,1,8,128]{4,3,2,1,0:T(8,128)(2,1)S(1)} %get-tuple-element.114), channel_id=1, source_target_pairs={{0,4},{4,8},{8,12},{12,16},{16,20},{20,24},{24,28},{28,32},{32,36}... | collective-permute-start | bytes 12296 | tf_op jit(solution)/shard_map/ppermute | solution.py:22
  10.9 50.2 %collective-permute-start = (bf16[2,1,1,8,128]{4,3,2,1,0:T(8,128)(2,1)S(1)}, bf16[2,1,1,8,128]{4,3,2,1,0:T(8,128)(2,1)S(1)}, u32[]{:S(2)}, u32[]{:S(2)}) collective-permute-start(bf16[2,1,1,8,128]{4,3,2,1,0:T(8,128)(2,1)S(1)} %get-tuple-element.115), channel_id=1, source_target_pairs={{0,4},{4,8},{8,12},{12,16},{16,20},{20,24},{24,28},{28,32},{32,36}... | collective-permute-start | bytes 12296 | tf_op jit(solution)/shard_map/ppermute | solution.py:22
  20.1 43.5 %collective-permute-start.7 = (bf16[2,1,1,8,128]{4,3,2,1,0:T(8,128)(2,1)S(1)}, bf16[2,1,1,8,128]{4,3,2,1,0:T(8,128)(2,1)S(1)}, u32[]{:S(2)}, u32[]{:S(2)}) collective-permute-start(bf16[2,1,1,8,128]{4,3,2,1,0:T(8,128)(2,1)S(1)} %get-tuple-element.112), channel_id=1, source_target_pairs={{4,0},{8,4},{12,8},{16,12},{20,16},{24,20},{28,24},{32,28},{36,32}... | collective-permute-start | bytes 12296 | tf_op jit(solution)/shard_map/ppermute | solution.py:22
  23.8 44.1 %collective-permute-start.10 = (bf16[2,1,1,8,128]{4,3,2,1,0:T(8,128)(2,1)S(1)}, bf16[2,1,1,8,128]{4,3,2,1,0:T(8,128)(2,1)S(1)}, u32[]{:S(2)}, u32[]{:S(2)}) collective-permute-start(bf16[2,1,1,8,128]{4,3,2,1,0:T(8,128)(2,1)S(1)} %get-tuple-element.113), channel_id=1, source_target_pairs={{4,0},{8,4},{12,8},{16,12},{20,16},{24,20},{28,24},{32,28},{36,32}... | collective-permute-start | bytes 12296 | tf_op jit(solution)/shard_map/ppermute | solution.py:22
  27.4 71.2 %collective-permute-start.31 = (bf16[2,1,1,4,256]{4,3,2,1,0:T(4,128)(2,1)S(1)}, bf16[2,1,1,4,256]{4,3,2,1,0:T(4,128)(2,1)S(1)}, u32[]{:S(2)}, u32[]{:S(2)}) collective-permute-start(bf16[2,1,1,4,256]{4,3,2,1,0:T(4,128)(2,1)S(1)} %get-tuple-element.148), channel_id=1, source_target_pairs={{4,0},{8,4},{12,8},{16,12},{20,16},{24,20},{28,24},{32,28},{36,32}... | collective-permute-start | bytes 12296 | tf_op jit(solution)/shard_map/ppermute | solution.py:22
  61.2 39.9 %collective-permute-start.34 = (bf16[2,1,1,4,256]{4,3,2,1,0:T(4,128)(2,1)S(1)}, bf16[2,1,1,4,256]{4,3,2,1,0:T(4,128)(2,1)S(1)}, u32[]{:S(2)}, u32[]{:S(2)}) collective-permute-start(bf16[2,1,1,4,256]{4,3,2,1,0:T(4,128)(2,1)S(1)} %get-tuple-element.149), channel_id=1, source_target_pairs={{4,0},{8,4},{12,8},{16,12},{20,16},{24,20},{28,24},{32,28},{36,32}... | collective-permute-start | bytes 12296 | tf_op jit(solution)/shard_map/ppermute | solution.py:22
  63.6 25.7 %collective-permute-start.1 = (bf16[2,1,1,8,128]{4,3,2,1,0:T(8,128)(2,1)S(1)}, bf16[2,1,1,8,128]{4,3,2,1,0:T(8,128)(2,1)S(1)}, u32[]{:S(2)}, u32[]{:S(2)}) collective-permute-start(bf16[2,1,1,8,128]{4,3,2,1,0:T(8,128)(2,1)S(1)} %collective-permute-done), channel_id=1, source_target_pairs={{0,1},{1,2},{2,3},{4,5},{5,6},{6,7},{8,9},{9,10},{10,11},{12,13},{... | collective-permute-start | bytes 12296 | tf_op jit(solution)/shard_map/ppermute | solution.py:22
  67.9 27.7 %collective-permute-start.8 = (bf16[2,1,1,8,128]{4,3,2,1,0:T(8,128)(2,1)S(1)}, bf16[2,1,1,8,128]{4,3,2,1,0:T(8,128)(2,1)S(1)}, u32[]{:S(2)}, u32[]{:S(2)}) collective-permute-start(bf16[2,1,1,8,128]{4,3,2,1,0:T(8,128)(2,1)S(1)} %collective-permute-done.7), channel_id=1, source_target_pairs={{0,1},{1,2},{2,3},{4,5},{5,6},{6,7},{8,9},{9,10},{10,11},{12,13},{... | collective-permute-start | bytes 12296 | tf_op jit(solution)/shard_map/ppermute | solution.py:22
  70.8 33.9 %collective-permute-start.11 = (bf16[2,1,1,8,128]{4,3,2,1,0:T(8,128)(2,1)S(1)}, bf16[2,1,1,8,128]{4,3,2,1,0:T(8,128)(2,1)S(1)}, u32[]{:S(2)}, u32[]{:S(2)}) collective-permute-start(bf16[2,1,1,8,128]{4,3,2,1,0:T(8,128)(2,1)S(1)} %collective-permute-done.10), channel_id=1, source_target_pairs={{1,0},{2,1},{3,2},{5,4},{6,5},{7,6},{9,8},{10,9},{11,10},{13,12},{... | collective-permute-start | bytes 12296 | tf_op jit(solution)/shard_map/ppermute | solution.py:22
  89.3 50.1 %collective-permute-start.29 = (bf16[2,4,1,4,256]{4,3,2,1,0:T(4,128)(2,1)S(1)}, bf16[2,4,1,4,256]{4,3,2,1,0:T(4,128)(2,1)S(1)}, u32[]{:S(2)}, u32[]{:S(2)}) collective-permute-start(bf16[2,4,1,4,256]{4,3,2,1,0:T(4,128)(2,1)S(1)} %get-tuple-element.154), channel_id=1, source_target_pairs={{0,1},{1,2},{2,3},{4,5},{5,6},{6,7},{8,9},{9,10},{10,11},{12,13},{... | collective-permute-start | bytes 49160 | tf_op jit(solution)/shard_map/ppermute | solution.py:22
  98.6 25.5 %collective-permute-start.24 = (bf16[2,1,1,4,256]{4,3,2,1,0:T(4,128)(2,1)S(1)}, bf16[2,1,1,4,256]{4,3,2,1,0:T(4,128)(2,1)S(1)}, u32[]{:S(2)}, u32[]{:S(2)}) collective-permute-start(bf16[2,1,1,4,256]{4,3,2,1,0:T(4,128)(2,1)S(1)} %get-tuple-element.151), channel_id=1, source_target_pairs={{0,4},{4,8},{8,12},{12,16},{16,20},{20,24},{24,28},{28,32},{32,36}... | collective-permute-start | bytes 12296 | tf_op jit(solution)/shard_map/ppermute | solution.py:22
  101.1 24.4 %collective-permute-start.32 = (bf16[2,1,1,4,256]{4,3,2,1,0:T(4,128)(2,1)S(1)}, bf16[2,1,1,4,256]{4,3,2,1,0:T(4,128)(2,1)S(1)}, u32[]{:S(2)}, u32[]{:S(2)}) collective-permute-start(bf16[2,1,1,4,256]{4,3,2,1,0:T(4,128)(2,1)S(1)} %collective-permute-done.31), channel_id=1, source_target_pairs={{0,1},{1,2},{2,3},{4,5},{5,6},{6,7},{8,9},{9,10},{10,11},{12,13},{... | collective-permute-start | bytes 12296 | tf_op jit(solution)/shard_map/ppermute | solution.py:22
  115.1 26.3 %collective-permute-start.33 = (bf16[2,1,4,4,256]{4,3,2,1,0:T(4,128)(2,1)S(1)}, bf16[2,1,4,4,256]{4,3,2,1,0:T(4,128)(2,1)S(1)}, u32[]{:S(2)}, u32[]{:S(2)}) collective-permute-start(bf16[2,1,4,4,256]{4,3,2,1,0:T(4,128)(2,1)S(1)} %get-tuple-element.152), channel_id=1, source_target_pairs={{4,0},{8,4},{12,8},{16,12},{20,16},{24,20},{28,24},{32,28},{36,32}... | collective-permute-start | bytes 49160 | tf_op jit(solution)/shard_map/ppermute | solution.py:22
  124.2 27.8 %collective-permute-start.30 = (bf16[2,4,1,4,256]{4,3,2,1,0:T(4,128)(2,1)S(1)}, bf16[2,4,1,4,256]{4,3,2,1,0:T(4,128)(2,1)S(1)}, u32[]{:S(2)}, u32[]{:S(2)}) collective-permute-start(bf16[2,4,1,4,256]{4,3,2,1,0:T(4,128)(2,1)S(1)} %get-tuple-element.155), channel_id=1, source_target_pairs={{1,0},{2,1},{3,2},{5,4},{6,5},{7,6},{9,8},{10,9},{11,10},{13,12},{... | collective-permute-start | bytes 49160 | tf_op jit(solution)/shard_map/ppermute | solution.py:22
  133.6 35.4 %collective-permute-start.6 = (bf16[2,8,1,8,128]{4,3,2,1,0:T(8,128)(2,1)S(1)}, bf16[2,8,1,8,128]{4,3,2,1,0:T(8,128)(2,1)S(1)}, u32[]{:S(2)}, u32[]{:S(2)}) collective-permute-start(bf16[2,8,1,8,128]{4,3,2,1,0:T(8,128)(2,1)S(1)} %get-tuple-element.119), channel_id=1, source_target_pairs={{1,0},{2,1},{3,2},{5,4},{6,5},{7,6},{9,8},{10,9},{11,10},{13,12},{... | collective-permute-start | bytes 98312 | tf_op jit(solution)/shard_map/ppermute | solution.py:22
  134.9 35.8 %collective-permute-start.5 = (bf16[2,8,1,8,128]{4,3,2,1,0:T(8,128)(2,1)S(1)}, bf16[2,8,1,8,128]{4,3,2,1,0:T(8,128)(2,1)S(1)}, u32[]{:S(2)}, u32[]{:S(2)}) collective-permute-start(bf16[2,8,1,8,128]{4,3,2,1,0:T(8,128)(2,1)S(1)} %get-tuple-element.118), channel_id=1, source_target_pairs={{0,1},{1,2},{2,3},{4,5},{5,6},{6,7},{8,9},{9,10},{10,11},{12,13},{... | collective-permute-start | bytes 98312 | tf_op jit(solution)/shard_map/ppermute | solution.py:22
  139.5 32.9 %collective-permute-start.2 = (bf16[2,1,8,8,128]{4,3,2,1,0:T(8,128)(2,1)S(1)}, bf16[2,1,8,8,128]{4,3,2,1,0:T(8,128)(2,1)S(1)}, u32[]{:S(2)}, u32[]{:S(2)}) collective-permute-start(bf16[2,1,8,8,128]{4,3,2,1,0:T(8,128)(2,1)S(1)} %get-tuple-element.117), channel_id=1, source_target_pairs={{0,4},{4,8},{8,12},{12,16},{16,20},{20,24},{24,28},{28,32},{32,36}... | collective-permute-start | bytes 98312 | tf_op jit(solution)/shard_map/ppermute | solution.py:22
  141.4 32.7 %collective-permute-start.9 = (bf16[2,1,8,8,128]{4,3,2,1,0:T(8,128)(2,1)S(1)}, bf16[2,1,8,8,128]{4,3,2,1,0:T(8,128)(2,1)S(1)}, u32[]{:S(2)}, u32[]{:S(2)}) collective-permute-start(bf16[2,1,8,8,128]{4,3,2,1,0:T(8,128)(2,1)S(1)} %get-tuple-element.116), channel_id=1, source_target_pairs={{4,0},{8,4},{12,8},{16,12},{20,16},{24,20},{28,24},{32,28},{36,32}... | collective-permute-start | bytes 98312 | tf_op jit(solution)/shard_map/ppermute | solution.py:22
  205.6 72.1 %collective-permute-start.17 = (bf16[2,4,1,4,256]{4,3,2,1,0:T(4,128)(2,1)S(1)}, bf16[2,4,1,4,256]{4,3,2,1,0:T(4,128)(2,1)S(1)}, u32[]{:S(2)}, u32[]{:S(2)}) collective-permute-start(bf16[2,4,1,4,256]{4,3,2,1,0:T(4,128)(2,1)S(1)} %get-tuple-element.164), channel_id=1, source_target_pairs={{0,1},{1,2},{2,3},{4,5},{5,6},{6,7},{8,9},{9,10},{10,11},{12,13},{... | collective-permute-start | bytes 49160 | tf_op jit(solution)/shard_map/ppermute | solution.py:22
  241.6 38.3 %collective-permute-start.21 = (bf16[2,1,4,4,256]{4,3,2,1,0:T(4,128)(2,1)S(1)}, bf16[2,1,4,4,256]{4,3,2,1,0:T(4,128)(2,1)S(1)}, u32[]{:S(2)}, u32[]{:S(2)}) collective-permute-start(bf16[2,1,4,4,256]{4,3,2,1,0:T(4,128)(2,1)S(1)} %get-tuple-element.160), channel_id=1, source_target_pairs={{4,0},{8,4},{12,8},{16,12},{20,16},{24,20},{28,24},{32,28},{36,32}... | collective-permute-start | bytes 49160 | tf_op jit(solution)/shard_map/ppermute | solution.py:22
  252.3 29.7 %collective-permute-start.18 = (bf16[2,4,1,4,256]{4,3,2,1,0:T(4,128)(2,1)S(1)}, bf16[2,4,1,4,256]{4,3,2,1,0:T(4,128)(2,1)S(1)}, u32[]{:S(2)}, u32[]{:S(2)}) collective-permute-start(bf16[2,4,1,4,256]{4,3,2,1,0:T(4,128)(2,1)S(1)} %get-tuple-element.165), channel_id=1, source_target_pairs={{1,0},{2,1},{3,2},{5,4},{6,5},{7,6},{9,8},{10,9},{11,10},{13,12},{... | collective-permute-start | bytes 49160 | tf_op jit(solution)/shard_map/ppermute | solution.py:22
  255.7 28.1 %collective-permute-start.14 = (bf16[2,1,4,4,256]{4,3,2,1,0:T(4,128)(2,1)S(1)}, bf16[2,1,4,4,256]{4,3,2,1,0:T(4,128)(2,1)S(1)}, u32[]{:S(2)}, u32[]{:S(2)}) collective-permute-start(bf16[2,1,4,4,256]{4,3,2,1,0:T(4,128)(2,1)S(1)} %get-tuple-element.161), channel_id=1, source_target_pairs={{0,4},{4,8},{8,12},{12,16},{16,20},{20,24},{24,28},{28,32},{32,36}... | collective-permute-start | bytes 49160 | tf_op jit(solution)/shard_map/ppermute | solution.py:22
  977.5 51.3 %collective-permute-start.45 = (bf16[2,1,8,8,128]{4,3,2,1,0:T(8,128)(2,1)S(1)}, bf16[2,1,8,8,128]{4,3,2,1,0:T(8,128)(2,1)S(1)}, u32[]{:S(2)}, u32[]{:S(2)}) collective-permute-start(bf16[2,1,8,8,128]{4,3,2,1,0:T(8,128)(2,1)S(1)} %copy-done.33), channel_id=1, source_target_pairs={{4,0},{8,4},{12,8},{16,12},{20,16},{24,20},{28,24},{32,28},{36,32}... | collective-permute-start | bytes 98312 | tf_op jit(solution)/shard_map/ppermute | solution.py:22
  (137 other events, 10271.7 us)
Sparse Core Ops, SparseCore 0:
  393.4 404.4 reduce-scatter.3
